TPU v7x, 256 devices: a whole 4x4x8 slice. The times are simulated.
256 devices in a mesh: leaf: 4 (over x), row: 4 (over y), col: 16 (over z, core).
Axes of the slice: x: 4, y: 4, z: 8, core: 2. Of those that a mesh axis runs over, the one named last changes fastest.
Arguments:
- local_inv: float32 [4, 4, 256, 128, 128], P('leaf', 'row', 'col'), may hold values from -2 to 2, as said below
- local_off: float32 [4, 4, 256, 2, 128, 128], P('leaf', 'row', 'col'), may hold values from -0.09375 to 0.09375
- local_dep: int32 [4, 4, 256, 2], P('leaf', 'row', 'col'), may hold values from 0 to 7
- local_rhs: float32 [4, 4, 256, 64, 128], P('leaf', 'row', 'col'), may hold values from -6 to 6
- top_inv: float32 [8, 4, 16, 128, 128], P(None, 'row', 'col'), may hold values from -2 to 2, as said below
- top_off: float32 [7, 4, 16, 4, 128, 128], P(None, 'row', 'col'), may hold values from -0.125 to 0.125
- top_dep: int32 [7, 4, 16, 4], P(None, 'row', 'col'), may hold values from 0 to 19
- top_rhs: float32 [8, 4, 16, 64, 128], P(None, 'row', 'col'), may hold values from -6 to 6
Outputs:
- local_sol: float32 [4, 4, 256, 64, 128], P('leaf', 'row', 'col')
- top_sol: float32 [8, 4, 16, 64, 128], P(None, 'row', 'col')
Inputs may be any that keep to these rules, and one draw needn't show every extreme that they name: `local_inv`: lower-triangular inverse diagonal blocks of a Cholesky factor: entry [t, s] is zero for s > t. `top_inv`: lower-triangular inverse diagonal blocks of a Cholesky factor: entry [t, s] is zero for s > t. `local_dep`: levels of ancestors owned by the supernode's own grid cell. `top_dep`: a value v < 16 names the supernode one level lower in cell (r, v); a value v >= 16 the one in cell (v - 16, c).
All inputs are finite; a program needn't handle non-finite values.
Results may differ from a plain program's by a relative error of at most 0.0001.
Values sent between devices are 32-bit elements; how exact they have to be, the bound alone decides.
No kernel may reach another device: no remote copies, remote signals or barrier semaphores. Data moves between devices by JAX's collectives and lax.ppermute only.
A program may use at most 64 MiB of HBM per device.

v0:
```python
import jax
import jax.numpy as jnp
from jax import lax
from jax.sharding import PartitionSpec as P

highest = lax.Precision.HIGHEST


def apply_inverse(inverse, block):
    return jnp.einsum("rs,ts->rt", block, inverse, precision=highest)


def apply_transpose(inverse, block):
    return jnp.einsum("rs,st->rt", block, inverse, precision=highest)


def shifted(value, axis, k):
    n = lax.axis_size(axis)
    return lax.ppermute(value, axis, [(i, (i + k) % n) for i in range(n)])


def select_sum(mask, stacked):
    mask = mask.reshape(mask.shape + (1,) * (stacked.ndim - 1))
    return jnp.sum(jnp.where(mask, stacked[None], 0.0), axis=1)


def spread_sum(mask, pieces):
    return jnp.sum(jnp.where(mask[:, :, None, None], pieces[:, None], 0.0), axis=0)


def gather_sources(block, col_pick, row_pick):
    by_col = lax.all_gather(block[None], "col", axis=0, tiled=True)
    n_row = lax.axis_size("row")
    by_shift = jnp.stack([block] + [shifted(block, "row", k) for k in range(1, n_row)])
    return select_sum(col_pick, by_col) + select_sum(row_pick, by_shift)


def push_back(pieces, col_pick, row_push):
    n_row = lax.axis_size("row")
    slots = spread_sum(col_pick, pieces)
    incoming = lax.all_to_all(slots, "col", 0, 0, tiled=True).sum(0)
    parts = spread_sum(row_push, pieces)
    incoming = incoming + parts[0]
    for k in range(1, n_row):
        incoming = incoming + shifted(parts[k], "row", k)
    return incoming


def solve_top(top_inverse, top_blocks, top_links, top_right, updates):
    levels = top_inverse.shape[0]
    width_cols = lax.axis_size("col")
    n_row = lax.axis_size("row")
    me_row = lax.axis_index("row")
    is_col = top_links < width_cols
    col_pick = top_links[..., None] == jnp.arange(width_cols, dtype=jnp.int32)
    pull = jnp.mod(me_row - (top_links - width_cols), n_row)
    push = jnp.mod(top_links - width_cols - me_row, n_row)
    shifts = jnp.arange(n_row, dtype=jnp.int32)
    row_pick = (~is_col)[..., None] & (pull[..., None] == shifts)
    row_push = (~is_col)[..., None] & (push[..., None] == shifts)
    forward = []
    for height in range(levels):
        target = top_right[height] - updates[height]
        if height > 0:
            picked = gather_sources(forward[-1], col_pick[height - 1], row_pick[height - 1])
            target = target - jnp.einsum(
                "jrs,jts->rt", picked, top_blocks[height - 1], precision=highest
            )
        forward.append(apply_inverse(top_inverse[height], target))
    forward = jnp.stack(forward)
    current = apply_transpose(top_inverse[levels - 1], forward[levels - 1])
    solved = jnp.zeros_like(forward).at[levels - 1].set(current)

    def step(i, carry):
        current, solved = carry
        height = levels - 2 - i
        at = lambda a: lax.dynamic_index_in_dim(a, height, 0, keepdims=False)
        pieces = jnp.einsum("rt,jts->jrs", current, at(top_blocks), precision=highest)
        incoming = push_back(pieces, at(col_pick), at(row_push))
        current = apply_transpose(at(top_inverse), at(forward) - incoming)
        return (current, lax.dynamic_update_index_in_dim(solved, current, height, 0))

    return lax.fori_loop(0, levels - 1, step, (current, solved))[1]


def on_device(local_inv, local_off, local_dep, local_rhs, top_inv, top_off, top_dep, top_rhs):
    inverse = local_inv[0, 0]
    blocks = local_off[0, 0]
    ancestor_levels = local_dep[0, 0]
    right_local = local_rhs[0, 0]
    levels = top_inv.shape[0]
    top_inverse = top_inv[:, 0, 0]
    top_blocks = top_off[:, 0, 0]
    top_links = top_dep[:, 0, 0]
    top_right = top_rhs[:, 0, 0]
    local_first = jnp.einsum("krs,kts->krt", right_local, inverse, precision=highest)
    contributions = jnp.einsum("krs,kjts->kjrt", local_first, blocks, precision=highest)
    level_matches = (ancestor_levels[:, :, None] == jnp.arange(levels, dtype=jnp.int32)).astype(
        jnp.float32
    )
    updates = jnp.einsum("kjl,kjrt->lrt", level_matches, contributions, precision=highest)
    n_leaf = lax.axis_size("leaf")
    by_shift = jnp.stack([updates] + [shifted(updates, "leaf", k) for k in range(1, n_leaf)])
    order = jnp.mod(lax.axis_index("leaf") - jnp.arange(n_leaf, dtype=jnp.int32), n_leaf)
    weights = order[:, None] == jnp.arange(n_leaf, dtype=jnp.int32)
    ordered = select_sum(weights, by_shift)
    totals = ordered[0]
    for u in range(1, n_leaf):
        totals = totals + ordered[u]
    top_solution = solve_top(top_inverse, top_blocks, top_links, top_right, totals)
    ancestors = jnp.einsum("kjl,lrt->kjrt", level_matches, top_solution, precision=highest)
    remainder = local_first - jnp.einsum("kjrt,kjts->krs", ancestors, blocks, precision=highest)
    local_solution = jnp.einsum("krs,kst->krt", remainder, inverse, precision=highest)
    return (local_solution[None, None], top_solution[:, None, None])


def solution(mesh):
    placed = (
        P("leaf", "row", "col", None, None),
        P("leaf", "row", "col", None, None, None),
        P("leaf", "row", "col", None),
        P("leaf", "row", "col", None, None),
        P(None, "row", "col", None, None),
        P(None, "row", "col", None, None, None),
        P(None, "row", "col", None),
        P(None, "row", "col", None, None),
    )
    return jax.shard_map(
        on_device,
        mesh=mesh,
        in_specs=placed,
        out_specs=(P("leaf", "row", "col", None, None), P(None, "row", "col", None, None)),
        check_vma=False,
    )
```

profile of v0, /device:TPU:1, one launch (start us, length us, event | category | flops | bytes accessed | tf_op | source)
XLA Modules:
  0.0 378.8 jit_solution(4697018135431169076)
XLA Ops:
  0.6 3.7 fusion.36
  4.3 2.3 fusion.18
  7.8 2.1 collective-permute-start.3
  9.9 2.4 collective-permute-start.4
  14.9 8.8 %collective-permute-done.4 = f32[8,64,128]{2,0,1:T(8,128)S(1)} collective-permute-done((f32[8,64,128]{2,0,1:T(8,128)S(1)}, f32[8,64,128]{2,0,1:T(8,128)S(1)}, u32[]{:S(2)}, u32[]{:S(2)}) %collective-permute-start.4) | collective-permute-done | bytes 262176 | tf_op jit(solution)/shard_map/ppermute | solution.py:19
  26.5 1.4 collective-permute-start.6
  27.9 2.6 collective-permute-start.7
  31.6 23.6 %all-gather = f32[1024,128]{1,0:T(8,128)S(1)} all-gather(f32[64,128]{1,0:T(8,128)S(1)} %get-tuple-element.254), channel_id=2, replica_groups=mesh['leaf'=4,'row'=4,'col'=16] {'col'}, dimensions={0}, use_global_device_ids=true | all-gather | bytes 557056 | tf_op jit(solution)/shard_map/all_gather | solution.py:32
  59.0 2.0 collective-permute-start.11
  61.0 16.3 %all-gather.1 = f32[1024,128]{1,0:T(8,128)S(1)} all-gather(f32[64,128]{1,0:T(8,128)S(1)} %get-tuple-element.256), channel_id=3, replica_groups=mesh['leaf'=4,'row'=4,'col'=16] {'col'}, dimensions={0}, use_global_device_ids=true | all-gather | bytes 557056 | tf_op jit(solution)/shard_map/all_gather | solution.py:32
  80.6 2.2 collective-permute-start.13
  82.7 2.0 collective-permute-start.14
  84.7 18.2 %all-gather.2 = f32[1024,128]{1,0:T(8,128)S(1)} all-gather(f32[64,128]{1,0:T(8,128)S(1)} %get-tuple-element.258), channel_id=4, replica_groups=mesh['leaf'=4,'row'=4,'col'=16] {'col'}, dimensions={0}, use_global_device_ids=true | all-gather | bytes 557056 | tf_op jit(solution)/shard_map/all_gather | solution.py:32
  106.8 1.8 collective-permute-start.17
  108.5 16.5 %all-gather.3 = f32[1024,128]{1,0:T(8,128)S(1)} all-gather(f32[64,128]{1,0:T(8,128)S(1)} %get-tuple-element.260), channel_id=5, replica_groups=mesh['leaf'=4,'row'=4,'col'=16] {'col'}, dimensions={0}, use_global_device_ids=true | all-gather | bytes 557056 | tf_op jit(solution)/shard_map/all_gather | solution.py:32
  128.3 2.2 collective-permute-start.19
  130.5 2.0 collective-permute-start.20
  132.4 18.2 %all-gather.4 = f32[1024,128]{1,0:T(8,128)S(1)} all-gather(f32[64,128]{1,0:T(8,128)S(1)} %get-tuple-element.262), channel_id=6, replica_groups=mesh['leaf'=4,'row'=4,'col'=16] {'col'}, dimensions={0}, use_global_device_ids=true | all-gather | bytes 557056 | tf_op jit(solution)/shard_map/all_gather | solution.py:32
  154.5 1.8 collective-permute-start.23
  156.3 16.7 %all-gather.5 = f32[1024,128]{1,0:T(8,128)S(1)} all-gather(f32[64,128]{1,0:T(8,128)S(1)} %get-tuple-element.264), channel_id=7, replica_groups=mesh['leaf'=4,'row'=4,'col'=16] {'col'}, dimensions={0}, use_global_device_ids=true | all-gather | bytes 557056 | tf_op jit(solution)/shard_map/all_gather | solution.py:32
  176.2 2.2 collective-permute-start.25
  178.4 2.0 collective-permute-start.26
  180.4 18.2 %all-gather.6 = f32[1024,128]{1,0:T(8,128)S(1)} all-gather(f32[64,128]{1,0:T(8,128)S(1)} %get-tuple-element.266), channel_id=8, replica_groups=mesh['leaf'=4,'row'=4,'col'=16] {'col'}, dimensions={0}, use_global_device_ids=true | all-gather | bytes 557056 | tf_op jit(solution)/shard_map/all_gather | solution.py:32
  203.3 170.0 %while.18 = (s32[]{:T(128)}, f32[64,128]{1,0:T(8,128)S(1)}, f32[8,64,128]{2,1,0:T(8,128)}, f32[8,64,128]{2,1,0:T(8,128)}, pred[7,4,16]{2,1,0:T(4,128)(4,1)S(1)},...) while((s32[]{:T(128)}, f32[64,128]{1,0:T(8,128)S(1)}, ...), condition=%wide.region_19.20_spmd, body=%wide.region_15.19_spmd.sunk | while | flops 64225288 | bytes 4393060 | solution.py:83
  205.5 3.8 %all-to-all-start = ((f32[16,64,128]{2,1,0:T(8,128)}), f32[16,64,128]{2,1,0:T(8,128)S(1)}, u32[]{:S(2)}, u32[]{:S(2)}) async-start(f32[16,64,128]{2,1,0:T(8,128)} %select_reduce_fusion.20), calls=%async_computation | async-start | bytes 1048576 | tf_op jit(solution)/shard_map/while/body/eval_jaxpr/all_to_all | solution.py:41
  211.0 15.5 %all-to-all-done = f32[16,64,128]{2,1,0:T(8,128)S(1)} async-done(((f32[16,64,128]{2,1,0:T(8,128)}), f32[16,64,128]{2,1,0:T(8,128)S(1)}, u32[]{:S(2)}, u32[]{:S(2)}) %all-to-all-start) | async-done | bytes 524320 | tf_op jit(solution)/shard_map/while/body/eval_jaxpr/all_to_all | solution.py:41
  226.6 1.7 bitcast_dynamic-update-slice_fusion.3
  230.5 3.5 all-to-all-start
  235.7 15.0 %all-to-all-done = f32[16,64,128]{2,1,0:T(8,128)S(1)} async-done(((f32[16,64,128]{2,1,0:T(8,128)}), f32[16,64,128]{2,1,0:T(8,128)S(1)}, u32[]{:S(2)}, u32[]{:S(2)}) %all-to-all-start) | async-done | bytes 524320 | tf_op jit(solution)/shard_map/while/body/eval_jaxpr/all_to_all | solution.py:41
  250.8 1.7 bitcast_dynamic-update-slice_fusion.3
  254.7 3.5 all-to-all-start
  259.9 15.0 %all-to-all-done = f32[16,64,128]{2,1,0:T(8,128)S(1)} async-done(((f32[16,64,128]{2,1,0:T(8,128)}), f32[16,64,128]{2,1,0:T(8,128)S(1)}, u32[]{:S(2)}, u32[]{:S(2)}) %all-to-all-start) | async-done | bytes 524320 | tf_op jit(solution)/shard_map/while/body/eval_jaxpr/all_to_all | solution.py:41
  274.9 1.7 bitcast_dynamic-update-slice_fusion.3
  278.9 3.5 all-to-all-start
  284.0 15.0 %all-to-all-done = f32[16,64,128]{2,1,0:T(8,128)S(1)} async-done(((f32[16,64,128]{2,1,0:T(8,128)}), f32[16,64,128]{2,1,0:T(8,128)S(1)}, u32[]{:S(2)}, u32[]{:S(2)}) %all-to-all-start) | async-done | bytes 524320 | tf_op jit(solution)/shard_map/while/body/eval_jaxpr/all_to_all | solution.py:41
  299.1 1.7 bitcast_dynamic-update-slice_fusion.3
  303.0 3.5 all-to-all-start
  308.2 15.0 %all-to-all-done = f32[16,64,128]{2,1,0:T(8,128)S(1)} async-done(((f32[16,64,128]{2,1,0:T(8,128)}), f32[16,64,128]{2,1,0:T(8,128)S(1)}, u32[]{:S(2)}, u32[]{:S(2)}) %all-to-all-start) | async-done | bytes 524320 | tf_op jit(solution)/shard_map/while/body/eval_jaxpr/all_to_all | solution.py:41
  323.3 1.7 bitcast_dynamic-update-slice_fusion.3
  327.2 3.5 all-to-all-start
  332.4 15.0 %all-to-all-done = f32[16,64,128]{2,1,0:T(8,128)S(1)} async-done(((f32[16,64,128]{2,1,0:T(8,128)}), f32[16,64,128]{2,1,0:T(8,128)S(1)}, u32[]{:S(2)}, u32[]{:S(2)}) %all-to-all-start) | async-done | bytes 524320 | tf_op jit(solution)/shard_map/while/body/eval_jaxpr/all_to_all | solution.py:41
  347.5 1.7 bitcast_dynamic-update-slice_fusion.3
  351.4 3.5 all-to-all-start
  356.5 15.0 %all-to-all-done = f32[16,64,128]{2,1,0:T(8,128)S(1)} async-done(((f32[16,64,128]{2,1,0:T(8,128)}), f32[16,64,128]{2,1,0:T(8,128)S(1)}, u32[]{:S(2)}, u32[]{:S(2)}) %all-to-all-start) | async-done | bytes 524320 | tf_op jit(solution)/shard_map/while/body/eval_jaxpr/all_to_all | solution.py:41
  371.6 1.7 bitcast_dynamic-update-slice_fusion.3
  373.3 1.6 fusion.49
  374.9 1.9 fusion.23
  376.9 1.9 convolution_bitcast_fusion.1
  (192 shorter events, 60.6 us)
Async XLA Ops:
  26.5 28.9 %collective-permute-start.6 = (f32[64,128]{1,0:T(8,128)S(1)}, f32[64,128]{1,0:T(8,128)S(1)}, u32[]{:S(2)}, u32[]{:S(2)}) collective-permute-start(f32[64,128]{1,0:T(8,128)S(1)} %get-tuple-element.254), channel_id=1, source_target_pairs={{0,16},{16,32},{32,48},{48,0},{1,17},{17,33},{33,49},{49,1},{2,18}... | collective-permute-start | bytes 98312 | tf_op jit(solution)/shard_map/ppermute | solution.py:19
  27.9 27.5 %collective-permute-start.7 = (f32[64,128]{1,0:T(8,128)S(1)}, f32[64,128]{1,0:T(8,128)S(1)}, u32[]{:S(2)}, u32[]{:S(2)}) collective-permute-start(f32[64,128]{1,0:T(8,128)S(1)} %get-tuple-element.254), channel_id=1, source_target_pairs={{0,32},{16,48},{32,0},{48,16},{1,33},{17,49},{33,1},{49,17},{2,34}... | collective-permute-start | bytes 98312 | tf_op jit(solution)/shard_map/ppermute | solution.py:19
  30.5 24.9 %collective-permute-start.8 = (f32[64,128]{1,0:T(8,128)S(1)}, f32[64,128]{1,0:T(8,128)S(1)}, u32[]{:S(2)}, u32[]{:S(2)}) collective-permute-start(f32[64,128]{1,0:T(8,128)S(1)} %get-tuple-element.254), channel_id=1, source_target_pairs={{0,48},{16,0},{32,16},{48,32},{1,49},{17,1},{33,17},{49,33},{2,50}... | collective-permute-start | bytes 98312 | tf_op jit(solution)/shard_map/ppermute | solution.py:19
  58.1 19.5 %collective-permute-start.9 = (f32[64,128]{1,0:T(8,128)S(1)}, f32[64,128]{1,0:T(8,128)S(1)}, u32[]{:S(2)}, u32[]{:S(2)}) collective-permute-start(f32[64,128]{1,0:T(8,128)S(1)} %get-tuple-element.256), channel_id=1, source_target_pairs={{0,16},{16,32},{32,48},{48,0},{1,17},{17,33},{33,49},{49,1},{2,18}... | collective-permute-start | bytes 98312 | tf_op jit(solution)/shard_map/ppermute | solution.py:19
  58.5 19.0 %collective-permute-start.10 = (f32[64,128]{1,0:T(8,128)S(1)}, f32[64,128]{1,0:T(8,128)S(1)}, u32[]{:S(2)}, u32[]{:S(2)}) collective-permute-start(f32[64,128]{1,0:T(8,128)S(1)} %get-tuple-element.256), channel_id=1, source_target_pairs={{0,32},{16,48},{32,0},{48,16},{1,33},{17,49},{33,1},{49,17},{2,34}... | collective-permute-start | bytes 98312 | tf_op jit(solution)/shard_map/ppermute | solution.py:19
  59.0 18.5 %collective-permute-start.11 = (f32[64,128]{1,0:T(8,128)S(1)}, f32[64,128]{1,0:T(8,128)S(1)}, u32[]{:S(2)}, u32[]{:S(2)}) collective-permute-start(f32[64,128]{1,0:T(8,128)S(1)} %get-tuple-element.256), channel_id=1, source_target_pairs={{0,48},{16,0},{32,16},{48,32},{1,49},{17,1},{33,17},{49,33},{2,50}... | collective-permute-start | bytes 98312 | tf_op jit(solution)/shard_map/ppermute | solution.py:19
  80.1 23.0 %collective-permute-start.12 = (f32[64,128]{1,0:T(8,128)S(1)}, f32[64,128]{1,0:T(8,128)S(1)}, u32[]{:S(2)}, u32[]{:S(2)}) collective-permute-start(f32[64,128]{1,0:T(8,128)S(1)} %get-tuple-element.258), channel_id=1, source_target_pairs={{0,16},{16,32},{32,48},{48,0},{1,17},{17,33},{33,49},{49,1},{2,18}... | collective-permute-start | bytes 98312 | tf_op jit(solution)/shard_map/ppermute | solution.py:19
  80.6 22.6 %collective-permute-start.13 = (f32[64,128]{1,0:T(8,128)S(1)}, f32[64,128]{1,0:T(8,128)S(1)}, u32[]{:S(2)}, u32[]{:S(2)}) collective-permute-start(f32[64,128]{1,0:T(8,128)S(1)} %get-tuple-element.258), channel_id=1, source_target_pairs={{0,32},{16,48},{32,0},{48,16},{1,33},{17,49},{33,1},{49,17},{2,34}... | collective-permute-start | bytes 98312 | tf_op jit(solution)/shard_map/ppermute | solution.py:19
  82.7 20.4 %collective-permute-start.14 = (f32[64,128]{1,0:T(8,128)S(1)}, f32[64,128]{1,0:T(8,128)S(1)}, u32[]{:S(2)}, u32[]{:S(2)}) collective-permute-start(f32[64,128]{1,0:T(8,128)S(1)} %get-tuple-element.258), channel_id=1, source_target_pairs={{0,48},{16,0},{32,16},{48,32},{1,49},{17,1},{33,17},{49,33},{2,50}... | collective-permute-start | bytes 98312 | tf_op jit(solution)/shard_map/ppermute | solution.py:19
  105.8 19.5 %collective-permute-start.15 = (f32[64,128]{1,0:T(8,128)S(1)}, f32[64,128]{1,0:T(8,128)S(1)}, u32[]{:S(2)}, u32[]{:S(2)}) collective-permute-start(f32[64,128]{1,0:T(8,128)S(1)} %get-tuple-element.260), channel_id=1, source_target_pairs={{0,16},{16,32},{32,48},{48,0},{1,17},{17,33},{33,49},{49,1},{2,18}... | collective-permute-start | bytes 98312 | tf_op jit(solution)/shard_map/ppermute | solution.py:19
  105.9 19.4 %collective-permute-start.16 = (f32[64,128]{1,0:T(8,128)S(1)}, f32[64,128]{1,0:T(8,128)S(1)}, u32[]{:S(2)}, u32[]{:S(2)}) collective-permute-start(f32[64,128]{1,0:T(8,128)S(1)} %get-tuple-element.260), channel_id=1, source_target_pairs={{0,32},{16,48},{32,0},{48,16},{1,33},{17,49},{33,1},{49,17},{2,34}... | collective-permute-start | bytes 98312 | tf_op jit(solution)/shard_map/ppermute | solution.py:19
  106.8 18.5 %collective-permute-start.17 = (f32[64,128]{1,0:T(8,128)S(1)}, f32[64,128]{1,0:T(8,128)S(1)}, u32[]{:S(2)}, u32[]{:S(2)}) collective-permute-start(f32[64,128]{1,0:T(8,128)S(1)} %get-tuple-element.260), channel_id=1, source_target_pairs={{0,48},{16,0},{32,16},{48,32},{1,49},{17,1},{33,17},{49,33},{2,50}... | collective-permute-start | bytes 98312 | tf_op jit(solution)/shard_map/ppermute | solution.py:19
  127.9 23.0 %collective-permute-start.18 = (f32[64,128]{1,0:T(8,128)S(1)}, f32[64,128]{1,0:T(8,128)S(1)}, u32[]{:S(2)}, u32[]{:S(2)}) collective-permute-start(f32[64,128]{1,0:T(8,128)S(1)} %get-tuple-element.262), channel_id=1, source_target_pairs={{0,16},{16,32},{32,48},{48,0},{1,17},{17,33},{33,49},{49,1},{2,18}... | collective-permute-start | bytes 98312 | tf_op jit(solution)/shard_map/ppermute | solution.py:19
  128.3 22.6 %collective-permute-start.19 = (f32[64,128]{1,0:T(8,128)S(1)}, f32[64,128]{1,0:T(8,128)S(1)}, u32[]{:S(2)}, u32[]{:S(2)}) collective-permute-start(f32[64,128]{1,0:T(8,128)S(1)} %get-tuple-element.262), channel_id=1, source_target_pairs={{0,32},{16,48},{32,0},{48,16},{1,33},{17,49},{33,1},{49,17},{2,34}... | collective-permute-start | bytes 98312 | tf_op jit(solution)/shard_map/ppermute | solution.py:19
  130.5 20.4 %collective-permute-start.20 = (f32[64,128]{1,0:T(8,128)S(1)}, f32[64,128]{1,0:T(8,128)S(1)}, u32[]{:S(2)}, u32[]{:S(2)}) collective-permute-start(f32[64,128]{1,0:T(8,128)S(1)} %get-tuple-element.262), channel_id=1, source_target_pairs={{0,48},{16,0},{32,16},{48,32},{1,49},{17,1},{33,17},{49,33},{2,50}... | collective-permute-start | bytes 98312 | tf_op jit(solution)/shard_map/ppermute | solution.py:19
  153.5 19.7 %collective-permute-start.21 = (f32[64,128]{1,0:T(8,128)S(1)}, f32[64,128]{1,0:T(8,128)S(1)}, u32[]{:S(2)}, u32[]{:S(2)}) collective-permute-start(f32[64,128]{1,0:T(8,128)S(1)} %get-tuple-element.264), channel_id=1, source_target_pairs={{0,16},{16,32},{32,48},{48,0},{1,17},{17,33},{33,49},{49,1},{2,18}... | collective-permute-start | bytes 98312 | tf_op jit(solution)/shard_map/ppermute | solution.py:19
  153.6 19.6 %collective-permute-start.22 = (f32[64,128]{1,0:T(8,128)S(1)}, f32[64,128]{1,0:T(8,128)S(1)}, u32[]{:S(2)}, u32[]{:S(2)}) collective-permute-start(f32[64,128]{1,0:T(8,128)S(1)} %get-tuple-element.264), channel_id=1, source_target_pairs={{0,32},{16,48},{32,0},{48,16},{1,33},{17,49},{33,1},{49,17},{2,34}... | collective-permute-start | bytes 98312 | tf_op jit(solution)/shard_map/ppermute | solution.py:19
  154.5 18.7 %collective-permute-start.23 = (f32[64,128]{1,0:T(8,128)S(1)}, f32[64,128]{1,0:T(8,128)S(1)}, u32[]{:S(2)}, u32[]{:S(2)}) collective-permute-start(f32[64,128]{1,0:T(8,128)S(1)} %get-tuple-element.264), channel_id=1, source_target_pairs={{0,48},{16,0},{32,16},{48,32},{1,49},{17,1},{33,17},{49,33},{2,50}... | collective-permute-start | bytes 98312 | tf_op jit(solution)/shard_map/ppermute | solution.py:19
  175.8 23.0 %collective-permute-start.24 = (f32[64,128]{1,0:T(8,128)S(1)}, f32[64,128]{1,0:T(8,128)S(1)}, u32[]{:S(2)}, u32[]{:S(2)}) collective-permute-start(f32[64,128]{1,0:T(8,128)S(1)} %get-tuple-element.266), channel_id=1, source_target_pairs={{0,16},{16,32},{32,48},{48,0},{1,17},{17,33},{33,49},{49,1},{2,18}... | collective-permute-start | bytes 98312 | tf_op jit(solution)/shard_map/ppermute | solution.py:19
  176.2 22.6 %collective-permute-start.25 = (f32[64,128]{1,0:T(8,128)S(1)}, f32[64,128]{1,0:T(8,128)S(1)}, u32[]{:S(2)}, u32[]{:S(2)}) collective-permute-start(f32[64,128]{1,0:T(8,128)S(1)} %get-tuple-element.266), channel_id=1, source_target_pairs={{0,32},{16,48},{32,0},{48,16},{1,33},{17,49},{33,1},{49,17},{2,34}... | collective-permute-start | bytes 98312 | tf_op jit(solution)/shard_map/ppermute | solution.py:19
  178.4 20.4 %collective-permute-start.26 = (f32[64,128]{1,0:T(8,128)S(1)}, f32[64,128]{1,0:T(8,128)S(1)}, u32[]{:S(2)}, u32[]{:S(2)}) collective-permute-start(f32[64,128]{1,0:T(8,128)S(1)} %get-tuple-element.266), channel_id=1, source_target_pairs={{0,48},{16,0},{32,16},{48,32},{1,49},{17,1},{33,17},{49,33},{2,50}... | collective-permute-start | bytes 98312 | tf_op jit(solution)/shard_map/ppermute | solution.py:19
  205.5 21.0 %all-to-all-start = ((f32[16,64,128]{2,1,0:T(8,128)}), f32[16,64,128]{2,1,0:T(8,128)S(1)}, u32[]{:S(2)}, u32[]{:S(2)}) async-start(f32[16,64,128]{2,1,0:T(8,128)} %select_reduce_fusion.20), calls=%async_computation | async-start | bytes 1048576 | tf_op jit(solution)/shard_map/while/body/eval_jaxpr/all_to_all | solution.py:41
  209.5 17.1 %collective-permute-start = (f32[64,128]{1,0:T(8,128)S(1)}, f32[64,128]{1,0:T(8,128)S(1)}, u32[]{:S(2)}, u32[]{:S(2)}) collective-permute-start(f32[64,128]{1,0:T(8,128)S(1)} %get-tuple-element.323), channel_id=1, source_target_pairs={{0,48},{16,0},{32,16},{48,32},{1,49},{17,1},{33,17},{49,33},{2,50}... | collective-permute-start | bytes 98312 | tf_op jit(solution)/shard_map/while/body/eval_jaxpr/ppermute | solution.py:19
  209.6 17.0 %collective-permute-start.1 = (f32[64,128]{1,0:T(8,128)S(1)}, f32[64,128]{1,0:T(8,128)S(1)}, u32[]{:S(2)}, u32[]{:S(2)}) collective-permute-start(f32[64,128]{1,0:T(8,128)S(1)} %get-tuple-element.324), channel_id=1, source_target_pairs={{0,32},{16,48},{32,0},{48,16},{1,33},{17,49},{33,1},{49,17},{2,34}... | collective-permute-start | bytes 98312 | tf_op jit(solution)/shard_map/while/body/eval_jaxpr/ppermute | solution.py:19
  210.6 16.1 %collective-permute-start.2 = (f32[64,128]{1,0:T(8,128)S(1)}, f32[64,128]{1,0:T(8,128)S(1)}, u32[]{:S(2)}, u32[]{:S(2)}) collective-permute-start(f32[64,128]{1,0:T(8,128)S(1)} %get-tuple-element.325), channel_id=1, source_target_pairs={{0,16},{16,32},{32,48},{48,0},{1,17},{17,33},{33,49},{49,1},{2,18}... | collective-permute-start | bytes 98312 | tf_op jit(solution)/shard_map/while/body/eval_jaxpr/ppermute | solution.py:19
  230.5 20.2 %all-to-all-start = ((f32[16,64,128]{2,1,0:T(8,128)}), f32[16,64,128]{2,1,0:T(8,128)S(1)}, u32[]{:S(2)}, u32[]{:S(2)}) async-start(f32[16,64,128]{2,1,0:T(8,128)} %select_reduce_fusion.20), calls=%async_computation | async-start | bytes 1048576 | tf_op jit(solution)/shard_map/while/body/eval_jaxpr/all_to_all | solution.py:41
  234.2 16.6 %collective-permute-start = (f32[64,128]{1,0:T(8,128)S(1)}, f32[64,128]{1,0:T(8,128)S(1)}, u32[]{:S(2)}, u32[]{:S(2)}) collective-permute-start(f32[64,128]{1,0:T(8,128)S(1)} %get-tuple-element.323), channel_id=1, source_target_pairs={{0,48},{16,0},{32,16},{48,32},{1,49},{17,1},{33,17},{49,33},{2,50}... | collective-permute-start | bytes 98312 | tf_op jit(solution)/shard_map/while/body/eval_jaxpr/ppermute | solution.py:19
  234.2 16.5 %collective-permute-start.1 = (f32[64,128]{1,0:T(8,128)S(1)}, f32[64,128]{1,0:T(8,128)S(1)}, u32[]{:S(2)}, u32[]{:S(2)}) collective-permute-start(f32[64,128]{1,0:T(8,128)S(1)} %get-tuple-element.324), channel_id=1, source_target_pairs={{0,32},{16,48},{32,0},{48,16},{1,33},{17,49},{33,1},{49,17},{2,34}... | collective-permute-start | bytes 98312 | tf_op jit(solution)/shard_map/while/body/eval_jaxpr/ppermute | solution.py:19
  254.7 20.2 %all-to-all-start = ((f32[16,64,128]{2,1,0:T(8,128)}), f32[16,64,128]{2,1,0:T(8,128)S(1)}, u32[]{:S(2)}, u32[]{:S(2)}) async-start(f32[16,64,128]{2,1,0:T(8,128)} %select_reduce_fusion.20), calls=%async_computation | async-start | bytes 1048576 | tf_op jit(solution)/shard_map/while/body/eval_jaxpr/all_to_all | solution.py:41
  258.3 16.6 %collective-permute-start = (f32[64,128]{1,0:T(8,128)S(1)}, f32[64,128]{1,0:T(8,128)S(1)}, u32[]{:S(2)}, u32[]{:S(2)}) collective-permute-start(f32[64,128]{1,0:T(8,128)S(1)} %get-tuple-element.323), channel_id=1, source_target_pairs={{0,48},{16,0},{32,16},{48,32},{1,49},{17,1},{33,17},{49,33},{2,50}... | collective-permute-start | bytes 98312 | tf_op jit(solution)/shard_map/while/body/eval_jaxpr/ppermute | solution.py:19
  258.4 16.5 %collective-permute-start.1 = (f32[64,128]{1,0:T(8,128)S(1)}, f32[64,128]{1,0:T(8,128)S(1)}, u32[]{:S(2)}, u32[]{:S(2)}) collective-permute-start(f32[64,128]{1,0:T(8,128)S(1)} %get-tuple-element.324), channel_id=1, source_target_pairs={{0,32},{16,48},{32,0},{48,16},{1,33},{17,49},{33,1},{49,17},{2,34}... | collective-permute-start | bytes 98312 | tf_op jit(solution)/shard_map/while/body/eval_jaxpr/ppermute | solution.py:19
  259.4 15.6 %collective-permute-start.2 = (f32[64,128]{1,0:T(8,128)S(1)}, f32[64,128]{1,0:T(8,128)S(1)}, u32[]{:S(2)}, u32[]{:S(2)}) collective-permute-start(f32[64,128]{1,0:T(8,128)S(1)} %get-tuple-element.325), channel_id=1, source_target_pairs={{0,16},{16,32},{32,48},{48,0},{1,17},{17,33},{33,49},{49,1},{2,18}... | collective-permute-start | bytes 98312 | tf_op jit(solution)/shard_map/while/body/eval_jaxpr/ppermute | solution.py:19
  278.9 20.2 %all-to-all-start = ((f32[16,64,128]{2,1,0:T(8,128)}), f32[16,64,128]{2,1,0:T(8,128)S(1)}, u32[]{:S(2)}, u32[]{:S(2)}) async-start(f32[16,64,128]{2,1,0:T(8,128)} %select_reduce_fusion.20), calls=%async_computation | async-start | bytes 1048576 | tf_op jit(solution)/shard_map/while/body/eval_jaxpr/all_to_all | solution.py:41
  282.5 16.6 %collective-permute-start = (f32[64,128]{1,0:T(8,128)S(1)}, f32[64,128]{1,0:T(8,128)S(1)}, u32[]{:S(2)}, u32[]{:S(2)}) collective-permute-start(f32[64,128]{1,0:T(8,128)S(1)} %get-tuple-element.323), channel_id=1, source_target_pairs={{0,48},{16,0},{32,16},{48,32},{1,49},{17,1},{33,17},{49,33},{2,50}... | collective-permute-start | bytes 98312 | tf_op jit(solution)/shard_map/while/body/eval_jaxpr/ppermute | solution.py:19
  282.6 16.5 %collective-permute-start.1 = (f32[64,128]{1,0:T(8,128)S(1)}, f32[64,128]{1,0:T(8,128)S(1)}, u32[]{:S(2)}, u32[]{:S(2)}) collective-permute-start(f32[64,128]{1,0:T(8,128)S(1)} %get-tuple-element.324), channel_id=1, source_target_pairs={{0,32},{16,48},{32,0},{48,16},{1,33},{17,49},{33,1},{49,17},{2,34}... | collective-permute-start | bytes 98312 | tf_op jit(solution)/shard_map/while/body/eval_jaxpr/ppermute | solution.py:19
  283.6 15.5 %collective-permute-start.2 = (f32[64,128]{1,0:T(8,128)S(1)}, f32[64,128]{1,0:T(8,128)S(1)}, u32[]{:S(2)}, u32[]{:S(2)}) collective-permute-start(f32[64,128]{1,0:T(8,128)S(1)} %get-tuple-element.325), channel_id=1, source_target_pairs={{0,16},{16,32},{32,48},{48,0},{1,17},{17,33},{33,49},{49,1},{2,18}... | collective-permute-start | bytes 98312 | tf_op jit(solution)/shard_map/while/body/eval_jaxpr/ppermute | solution.py:19
  303.0 20.2 %all-to-all-start = ((f32[16,64,128]{2,1,0:T(8,128)}), f32[16,64,128]{2,1,0:T(8,128)S(1)}, u32[]{:S(2)}, u32[]{:S(2)}) async-start(f32[16,64,128]{2,1,0:T(8,128)} %select_reduce_fusion.20), calls=%async_computation | async-start | bytes 1048576 | tf_op jit(solution)/shard_map/while/body/eval_jaxpr/all_to_all | solution.py:41
  306.6 16.6 %collective-permute-start = (f32[64,128]{1,0:T(8,128)S(1)}, f32[64,128]{1,0:T(8,128)S(1)}, u32[]{:S(2)}, u32[]{:S(2)}) collective-permute-start(f32[64,128]{1,0:T(8,128)S(1)} %get-tuple-element.323), channel_id=1, source_target_pairs={{0,48},{16,0},{32,16},{48,32},{1,49},{17,1},{33,17},{49,33},{2,50}... | collective-permute-start | bytes 98312 | tf_op jit(solution)/shard_map/while/body/eval_jaxpr/ppermute | solution.py:19
  306.7 16.5 %collective-permute-start.1 = (f32[64,128]{1,0:T(8,128)S(1)}, f32[64,128]{1,0:T(8,128)S(1)}, u32[]{:S(2)}, u32[]{:S(2)}) collective-permute-start(f32[64,128]{1,0:T(8,128)S(1)} %get-tuple-element.324), channel_id=1, source_target_pairs={{0,32},{16,48},{32,0},{48,16},{1,33},{17,49},{33,1},{49,17},{2,34}... | collective-permute-start | bytes 98312 | tf_op jit(solution)/shard_map/while/body/eval_jaxpr/ppermute | solution.py:19
  307.7 15.5 %collective-permute-start.2 = (f32[64,128]{1,0:T(8,128)S(1)}, f32[64,128]{1,0:T(8,128)S(1)}, u32[]{:S(2)}, u32[]{:S(2)}) collective-permute-start(f32[64,128]{1,0:T(8,128)S(1)} %get-tuple-element.325), channel_id=1, source_target_pairs={{0,16},{16,32},{32,48},{48,0},{1,17},{17,33},{33,49},{49,1},{2,18}... | collective-permute-start | bytes 98312 | tf_op jit(solution)/shard_map/while/body/eval_jaxpr/ppermute | solution.py:19
  327.2 20.2 %all-to-all-start = ((f32[16,64,128]{2,1,0:T(8,128)}), f32[16,64,128]{2,1,0:T(8,128)S(1)}, u32[]{:S(2)}, u32[]{:S(2)}) async-start(f32[16,64,128]{2,1,0:T(8,128)} %select_reduce_fusion.20), calls=%async_computation | async-start | bytes 1048576 | tf_op jit(solution)/shard_map/while/body/eval_jaxpr/all_to_all | solution.py:41
  330.8 16.6 %collective-permute-start = (f32[64,128]{1,0:T(8,128)S(1)}, f32[64,128]{1,0:T(8,128)S(1)}, u32[]{:S(2)}, u32[]{:S(2)}) collective-permute-start(f32[64,128]{1,0:T(8,128)S(1)} %get-tuple-element.323), channel_id=1, source_target_pairs={{0,48},{16,0},{32,16},{48,32},{1,49},{17,1},{33,17},{49,33},{2,50}... | collective-permute-start | bytes 98312 | tf_op jit(solution)/shard_map/while/body/eval_jaxpr/ppermute | solution.py:19
  330.9 16.5 %collective-permute-start.1 = (f32[64,128]{1,0:T(8,128)S(1)}, f32[64,128]{1,0:T(8,128)S(1)}, u32[]{:S(2)}, u32[]{:S(2)}) collective-permute-start(f32[64,128]{1,0:T(8,128)S(1)} %get-tuple-element.324), channel_id=1, source_target_pairs={{0,32},{16,48},{32,0},{48,16},{1,33},{17,49},{33,1},{49,17},{2,34}... | collective-permute-start | bytes 98312 | tf_op jit(solution)/shard_map/while/body/eval_jaxpr/ppermute | solution.py:19
  331.9 15.5 %collective-permute-start.2 = (f32[64,128]{1,0:T(8,128)S(1)}, f32[64,128]{1,0:T(8,128)S(1)}, u32[]{:S(2)}, u32[]{:S(2)}) collective-permute-start(f32[64,128]{1,0:T(8,128)S(1)} %get-tuple-element.325), channel_id=1, source_target_pairs={{0,16},{16,32},{32,48},{48,0},{1,17},{17,33},{33,49},{49,1},{2,18}... | collective-permute-start | bytes 98312 | tf_op jit(solution)/shard_map/while/body/eval_jaxpr/ppermute | solution.py:19
  351.4 20.2 %all-to-all-start = ((f32[16,64,128]{2,1,0:T(8,128)}), f32[16,64,128]{2,1,0:T(8,128)S(1)}, u32[]{:S(2)}, u32[]{:S(2)}) async-start(f32[16,64,128]{2,1,0:T(8,128)} %select_reduce_fusion.20), calls=%async_computation | async-start | bytes 1048576 | tf_op jit(solution)/shard_map/while/body/eval_jaxpr/all_to_all | solution.py:41
  355.0 16.6 %collective-permute-start = (f32[64,128]{1,0:T(8,128)S(1)}, f32[64,128]{1,0:T(8,128)S(1)}, u32[]{:S(2)}, u32[]{:S(2)}) collective-permute-start(f32[64,128]{1,0:T(8,128)S(1)} %get-tuple-element.323), channel_id=1, source_target_pairs={{0,48},{16,0},{32,16},{48,32},{1,49},{17,1},{33,17},{49,33},{2,50}... | collective-permute-start | bytes 98312 | tf_op jit(solution)/shard_map/while/body/eval_jaxpr/ppermute | solution.py:19
  355.1 16.5 %collective-permute-start.1 = (f32[64,128]{1,0:T(8,128)S(1)}, f32[64,128]{1,0:T(8,128)S(1)}, u32[]{:S(2)}, u32[]{:S(2)}) collective-permute-start(f32[64,128]{1,0:T(8,128)S(1)} %get-tuple-element.324), channel_id=1, source_target_pairs={{0,32},{16,48},{32,0},{48,16},{1,33},{17,49},{33,1},{49,17},{2,34}... | collective-permute-start | bytes 98312 | tf_op jit(solution)/shard_map/while/body/eval_jaxpr/ppermute | solution.py:19
  356.1 15.6 %collective-permute-start.2 = (f32[64,128]{1,0:T(8,128)S(1)}, f32[64,128]{1,0:T(8,128)S(1)}, u32[]{:S(2)}, u32[]{:S(2)}) collective-permute-start(f32[64,128]{1,0:T(8,128)S(1)} %get-tuple-element.325), channel_id=1, source_target_pairs={{0,16},{16,32},{32,48},{48,0},{1,17},{17,33},{33,49},{49,1},{2,18}... | collective-permute-start | bytes 98312 | tf_op jit(solution)/shard_map/while/body/eval_jaxpr/ppermute | solution.py:19
  (10 other events, 97.1 us)
where the time goes:
time: 381 us; the launch traced here: 379 us
  blocking collectives  128 us (34%)
  waiting for transfers between devices  115 us (30%)
  starting transfers between devices  68.4 us (18%)
  matrix products  52.2 us (14%)
  other arithmetic  11.9 us (3%)
    all_gather x7, blocking collectives, gather_sources(): by_col = lax.all_gather(block[None], 'col', axis=0, tiled=True)  128 us
    all_to_all x7, waiting for transfers between devices, push_back(): incoming = lax.all_to_all(slots, 'col', 0, 0, tiled=True).sum(0)  106 us
    ppermute x45, starting transfers between devices, shifted(): return lax.ppermute(value, axis, [(i, (i + k) % n) for i in range(n)])  43.7 us
    all_to_all x7, starting transfers between devices, push_back(): incoming = lax.all_to_all(slots, 'col', 0, 0, tiled=True).sum(0)  24.6 us
    dot_general x8, matrix products, apply_transpose(): return jnp.einsum('rs,st->rt', block, inverse, precision=highest)  12.8 us
    ppermute x45, waiting for transfers between devices, shifted(): return lax.ppermute(value, axis, [(i, (i + k) % n) for i in range(n)])  9.6 us
    dot_general x7, matrix products, solve_top(): jnp.einsum('jrs,jts->rt', picked, top_blocks[height - 1], precision=highest)  9.58 us
    dot_general x8, matrix products, apply_inverse(): return jnp.einsum('rs,ts->rt', block, inverse, precision=highest)  8.76 us
  transfers between devices with their start and end apart: 52, of which 9 were waited for; matrix products, arithmetic and copies ran while one was open for 1% of the time, Pallas kernels for 0%

commit v1 on v0

--- a/solution.py
+++ b/solution.py
@@ -4,6 +4,12 @@
 from jax.sharding import PartitionSpec as P
 
 highest = lax.Precision.HIGHEST
+
+
+def save_the_frame(body, net_axis, join_dim):
+    u_next = tuple((body for _ in range(lax.axis_size(net_axis))))
+    z_new = lax.all_to_all(jnp.stack(u_next), net_axis, 0, 0)
+    return jnp.concatenate(z_new, join_dim)
 
 
 def apply_inverse(inverse, block):
@@ -29,7 +35,7 @@
 
 
 def gather_sources(block, col_pick, row_pick):
-    by_col = lax.all_gather(block[None], "col", axis=0, tiled=True)
+    by_col = save_the_frame(block[None], "col", 0)
     n_row = lax.axis_size("row")
     by_shift = jnp.stack([block] + [shifted(block, "row", k) for k in range(1, n_row)])
     return select_sum(col_pick, by_col) + select_sum(row_pick, by_shift)

time: 381 us -> 388 us (1.018)
  blocking collectives: 128 us -> 0 us
  waiting for transfers between devices: 115 us -> 175 us
  starting transfers between devices: 68.4 us -> 123 us
  other arithmetic: 11.9 us -> 19.8 us
  local copies, waits for them, and re-layouts: 1.48 us -> 8.58 us
  matrix products: 52.2 us -> 56.8 us
    all_gather x7 -> x0, blocking collectives: 128 us -> none  [gather_sources(): by_col = lax.all_gather(block[None], 'col', axis=0, tiled=True)]
    all_to_all x0 -> x7, waiting for transfers between devices: none -> 63 us  [save_the_frame(): z_new = lax.all_to_all(jnp.stack(u_next), net_axis, 0, 0)]
    all_to_all x0 -> x7, starting transfers between devices: none -> 30.8 us  [save_the_frame(): z_new = lax.all_to_all(jnp.stack(u_next), net_axis, 0, 0)]
    ppermute x45, starting transfers between devices: 43.7 us -> 68.1 us  [shifted(): return lax.ppermute(value, axis, [(i, (i + k) % n) for i in range(n)])]
    all_to_all x7, waiting for transfers between devices: 106 us -> 89 us  [push_back(): incoming = lax.all_to_all(slots, 'col', 0, 0, tiled=True).sum(0)]
    ppermute x45, waiting for transfers between devices: 9.6 us -> 23.2 us  [shifted(): return lax.ppermute(value, axis, [(i, (i + k) % n) for i in range(n)])]
    reduce_sum x15, other arithmetic: 2.55 us -> 10.4 us  [select_sum(): return jnp.sum(jnp.where(mask, stacked[None], 0.0), axis=1)]
    another operation x0 -> x7, local copies, waits for them, and re-layouts: none -> 5.91 us  [save_the_frame(): z_new = lax.all_to_all(jnp.stack(u_next), net_axis, 0, 0)]
  transfers between devices with their start and end apart: 52 -> 59, of which waited for: 9 -> 30; matrix products, arithmetic and copies ran while one was open for 1% -> 2% of each run, Pallas kernels for 0% -> 0%
where the time goes in v1:
time: 388 us; the launch traced here: 385 us
  waiting for transfers between devices  175 us (45%)
  starting transfers between devices  123 us (32%)
  matrix products  56.8 us (15%)
  other arithmetic  19.8 us (5%)
  local copies, waits for them, and re-layouts  8.58 us (2%)
    all_to_all x7, waiting for transfers between devices, push_back(): incoming = lax.all_to_all(slots, 'col', 0, 0, tiled=True).sum(0)  89 us
    ppermute x45, starting transfers between devices, shifted(): return lax.ppermute(value, axis, [(i, (i + k) % n) for i in range(n)])  68.1 us
    all_to_all x7, waiting for transfers between devices, save_the_frame(): z_new = lax.all_to_all(jnp.stack(u_next), net_axis, 0, 0)  63 us
    all_to_all x7, starting transfers between devices, save_the_frame(): z_new = lax.all_to_all(jnp.stack(u_next), net_axis, 0, 0)  30.8 us
    all_to_all x7, starting transfers between devices, push_back(): incoming = lax.all_to_all(slots, 'col', 0, 0, tiled=True).sum(0)  24.3 us
    ppermute x45, waiting for transfers between devices, shifted(): return lax.ppermute(value, axis, [(i, (i + k) % n) for i in range(n)])  23.2 us
    dot_general x8, matrix products, apply_inverse(): return jnp.einsum('rs,ts->rt', block, inverse, precision=highest)  13.6 us
    dot_general x8, matrix products, apply_transpose(): return jnp.einsum('rs,st->rt', block, inverse, precision=highest)  12.7 us
  transfers between devices with their start and end apart: 59, of which 30 were waited for; matrix products, arithmetic and copies ran while one was open for 2% of the time, Pallas kernels for 0%

profile of v1, /device:TPU:1, one launch (start us, length us, event | category | flops | bytes accessed | tf_op | source)
XLA Modules:
  0.0 385.1 jit_solution(2503083402978063796)
XLA Ops:
  0.6 3.7 fusion.37
  4.3 2.3 fusion.20
  7.8 2.1 collective-permute-start.3
  9.9 2.4 collective-permute-start.4
  14.9 8.8 %collective-permute-done.4 = f32[8,64,128]{2,0,1:T(8,128)S(1)} collective-permute-done((f32[8,64,128]{2,0,1:T(8,128)S(1)}, f32[8,64,128]{2,0,1:T(8,128)S(1)}, u32[]{:S(2)}, u32[]{:S(2)}) %collective-permute-start.4) | collective-permute-done | bytes 262176 | tf_op jit(solution)/shard_map/ppermute | solution.py:25
  27.9 10.0 %all-to-all-start.1 = ((f32[16,1,64,128]{3,2,1,0:T(8,128)}), f32[16,1,64,128]{3,2,1,0:T(8,128)S(1)}, u32[]{:S(2)}, u32[]{:S(2)}) async-start(f32[16,1,64,128]{3,2,1,0:T(8,128)} %stack.159), calls=%async_computation.1 | async-start | bytes 1048576 | tf_op jit(solution)/shard_map/all_to_all | solution.py:11
  40.1 2.6 collective-permute-start.7
  45.9 9.2 %all-to-all-done.1 = f32[16,1,64,128]{3,2,1,0:T(8,128)S(1)} async-done(((f32[16,1,64,128]{3,2,1,0:T(8,128)}), f32[16,1,64,128]{3,2,1,0:T(8,128)S(1)}, u32[]{:S(2)}, u32[]{:S(2)}) %all-to-all-start.1) | async-done | bytes 524320 | tf_op jit(solution)/shard_map/all_to_all | solution.py:11
  59.9 3.5 all-to-all-start.2
  64.7 2.6 collective-permute-start.10
  71.2 8.8 %all-to-all-done.2 = f32[16,1,64,128]{3,2,1,0:T(8,128)S(1)} async-done(((f32[16,1,64,128]{3,2,1,0:T(8,128)}), f32[16,1,64,128]{3,2,1,0:T(8,128)S(1)}, u32[]{:S(2)}, u32[]{:S(2)}) %all-to-all-start.2) | async-done | bytes 524320 | tf_op jit(solution)/shard_map/all_to_all | solution.py:11
  84.8 3.5 all-to-all-start.3
  89.7 2.6 collective-permute-start.13
  96.1 8.9 %all-to-all-done.3 = f32[16,1,64,128]{3,2,1,0:T(8,128)S(1)} async-done(((f32[16,1,64,128]{3,2,1,0:T(8,128)}), f32[16,1,64,128]{3,2,1,0:T(8,128)S(1)}, u32[]{:S(2)}, u32[]{:S(2)}) %all-to-all-start.3) | async-done | bytes 524320 | tf_op jit(solution)/shard_map/all_to_all | solution.py:11
  109.7 3.5 all-to-all-start.4
  114.6 2.6 collective-permute-start.16
  121.1 8.9 %all-to-all-done.4 = f32[16,1,64,128]{3,2,1,0:T(8,128)S(1)} async-done(((f32[16,1,64,128]{3,2,1,0:T(8,128)}), f32[16,1,64,128]{3,2,1,0:T(8,128)S(1)}, u32[]{:S(2)}, u32[]{:S(2)}) %all-to-all-start.4) | async-done | bytes 524320 | tf_op jit(solution)/shard_map/all_to_all | solution.py:11
  134.7 3.5 all-to-all-start.5
  139.5 2.6 collective-permute-start.19
  146.0 8.8 %all-to-all-done.5 = f32[16,1,64,128]{3,2,1,0:T(8,128)S(1)} async-done(((f32[16,1,64,128]{3,2,1,0:T(8,128)}), f32[16,1,64,128]{3,2,1,0:T(8,128)S(1)}, u32[]{:S(2)}, u32[]{:S(2)}) %all-to-all-start.5) | async-done | bytes 524320 | tf_op jit(solution)/shard_map/all_to_all | solution.py:11
  159.7 3.5 all-to-all-start.6
  164.5 2.6 collective-permute-start.22
  170.9 8.9 %all-to-all-done.6 = f32[16,1,64,128]{3,2,1,0:T(8,128)S(1)} async-done(((f32[16,1,64,128]{3,2,1,0:T(8,128)}), f32[16,1,64,128]{3,2,1,0:T(8,128)S(1)}, u32[]{:S(2)}, u32[]{:S(2)}) %all-to-all-start.6) | async-done | bytes 524320 | tf_op jit(solution)/shard_map/all_to_all | solution.py:11
  184.6 3.5 all-to-all-start.7
  189.4 2.6 collective-permute-start.25
  195.2 9.5 %all-to-all-done.7 = f32[16,1,64,128]{3,2,1,0:T(8,128)S(1)} async-done(((f32[16,1,64,128]{3,2,1,0:T(8,128)}), f32[16,1,64,128]{3,2,1,0:T(8,128)S(1)}, u32[]{:S(2)}, u32[]{:S(2)}) %all-to-all-start.7) | async-done | bytes 524320 | tf_op jit(solution)/shard_map/all_to_all | solution.py:11
  210.4 169.2 %while.18 = (s32[]{:T(128)}, f32[64,128]{1,0:T(8,128)S(1)}, f32[8,64,128]{2,1,0:T(8,128)}, f32[8,64,128]{2,1,0:T(8,128)}, pred[7,4,16]{2,1,0:T(4,128)(4,1)S(1)},...) while((s32[]{:T(128)}, f32[64,128]{1,0:T(8,128)S(1)}, ...), condition=%wide.region_19.20_spmd, body=%wide.region_15.19_spmd.sunk | while | flops 64225288 | bytes 4393060 | solution.py:89
  212.7 3.5 all-to-all-start
  216.3 2.8 collective-permute-start
  220.2 12.7 %all-to-all-done = f32[16,64,128]{2,1,0:T(8,128)S(1)} async-done(((f32[16,64,128]{2,1,0:T(8,128)}), f32[16,64,128]{2,1,0:T(8,128)S(1)}, u32[]{:S(2)}, u32[]{:S(2)}) %all-to-all-start) | async-done | bytes 524320 | tf_op jit(solution)/shard_map/while/body/eval_jaxpr/all_to_all | solution.py:47
  236.9 3.5 all-to-all-start
  240.5 2.8 collective-permute-start
  244.3 12.7 %all-to-all-done = f32[16,64,128]{2,1,0:T(8,128)S(1)} async-done(((f32[16,64,128]{2,1,0:T(8,128)}), f32[16,64,128]{2,1,0:T(8,128)S(1)}, u32[]{:S(2)}, u32[]{:S(2)}) %all-to-all-start) | async-done | bytes 524320 | tf_op jit(solution)/shard_map/while/body/eval_jaxpr/all_to_all | solution.py:47
  261.0 3.5 all-to-all-start
  264.7 2.8 collective-permute-start
  268.5 12.7 %all-to-all-done = f32[16,64,128]{2,1,0:T(8,128)S(1)} async-done(((f32[16,64,128]{2,1,0:T(8,128)}), f32[16,64,128]{2,1,0:T(8,128)S(1)}, u32[]{:S(2)}, u32[]{:S(2)}) %all-to-all-start) | async-done | bytes 524320 | tf_op jit(solution)/shard_map/while/body/eval_jaxpr/all_to_all | solution.py:47
  285.2 3.5 all-to-all-start
  288.8 2.8 collective-permute-start
  292.7 12.7 %all-to-all-done = f32[16,64,128]{2,1,0:T(8,128)S(1)} async-done(((f32[16,64,128]{2,1,0:T(8,128)}), f32[16,64,128]{2,1,0:T(8,128)S(1)}, u32[]{:S(2)}, u32[]{:S(2)}) %all-to-all-start) | async-done | bytes 524320 | tf_op jit(solution)/shard_map/while/body/eval_jaxpr/all_to_all | solution.py:47
  309.4 3.5 all-to-all-start
  313.0 2.8 collective-permute-start
  316.9 12.7 %all-to-all-done = f32[16,64,128]{2,1,0:T(8,128)S(1)} async-done(((f32[16,64,128]{2,1,0:T(8,128)}), f32[16,64,128]{2,1,0:T(8,128)S(1)}, u32[]{:S(2)}, u32[]{:S(2)}) %all-to-all-start) | async-done | bytes 524320 | tf_op jit(solution)/shard_map/while/body/eval_jaxpr/all_to_all | solution.py:47
  333.6 3.5 all-to-all-start
  337.2 2.8 collective-permute-start
  341.0 12.7 %all-to-all-done = f32[16,64,128]{2,1,0:T(8,128)S(1)} async-done(((f32[16,64,128]{2,1,0:T(8,128)}), f32[16,64,128]{2,1,0:T(8,128)S(1)}, u32[]{:S(2)}, u32[]{:S(2)}) %all-to-all-start) | async-done | bytes 524320 | tf_op jit(solution)/shard_map/while/body/eval_jaxpr/all_to_all | solution.py:47
  357.7 3.5 all-to-all-start
  361.4 2.8 collective-permute-start
  365.2 12.7 %all-to-all-done = f32[16,64,128]{2,1,0:T(8,128)S(1)} async-done(((f32[16,64,128]{2,1,0:T(8,128)}), f32[16,64,128]{2,1,0:T(8,128)S(1)}, u32[]{:S(2)}, u32[]{:S(2)}) %all-to-all-start) | async-done | bytes 524320 | tf_op jit(solution)/shard_map/while/body/eval_jaxpr/all_to_all | solution.py:47
  (202 shorter events, 119.1 us)
Async XLA Ops:
  7.8 7.1 %collective-permute-start.3 = (f32[8,64,128]{2,0,1:T(8,128)S(1)}, f32[8,64,128]{2,0,1:T(8,128)S(1)}, u32[]{:S(2)}, u32[]{:S(2)}) collective-permute-start(f32[8,64,128]{2,0,1:T(8,128)S(1)} %bitcast.378), channel_id=1, source_target_pairs={{0,64},{64,128},{128,192},{192,0},{1,65},{65,129},{129,193},{193,1... | collective-permute-start | bytes 786440 | tf_op jit(solution)/shard_map/ppermute | solution.py:25
  9.9 13.8 %collective-permute-start.4 = (f32[8,64,128]{2,0,1:T(8,128)S(1)}, f32[8,64,128]{2,0,1:T(8,128)S(1)}, u32[]{:S(2)}, u32[]{:S(2)}) collective-permute-start(f32[8,64,128]{2,0,1:T(8,128)S(1)} %bitcast.379), channel_id=1, source_target_pairs={{0,128},{64,192},{128,0},{192,64},{1,129},{65,193},{129,1},{193,65... | collective-permute-start | bytes 786440 | tf_op jit(solution)/shard_map/ppermute | solution.py:25
  12.3 11.3 %collective-permute-start.5 = (f32[8,64,128]{2,0,1:T(8,128)S(1)}, f32[8,64,128]{2,0,1:T(8,128)}, u32[]{:S(2)}, u32[]{:S(2)}) collective-permute-start(f32[8,64,128]{2,0,1:T(8,128)S(1)} %bitcast.380), channel_id=1, source_target_pairs={{0,192},{64,0},{128,64},{192,128},{1,193},{65,1},{129,65},{193,129... | collective-permute-start | bytes 786440 | tf_op jit(solution)/shard_map/ppermute | solution.py:25
  27.9 27.2 %all-to-all-start.1 = ((f32[16,1,64,128]{3,2,1,0:T(8,128)}), f32[16,1,64,128]{3,2,1,0:T(8,128)S(1)}, u32[]{:S(2)}, u32[]{:S(2)}) async-start(f32[16,1,64,128]{3,2,1,0:T(8,128)} %stack.159), calls=%async_computation.1 | async-start | bytes 1048576 | tf_op jit(solution)/shard_map/all_to_all | solution.py:11
  38.8 5.7 %collective-permute-start.6 = (f32[64,128]{1,0:T(8,128)S(1)}, f32[64,128]{1,0:T(8,128)S(1)}, u32[]{:S(2)}, u32[]{:S(2)}) collective-permute-start(f32[64,128]{1,0:T(8,128)S(1)} %get-tuple-element.254), channel_id=1, source_target_pairs={{0,16},{16,32},{32,48},{48,0},{1,17},{17,33},{33,49},{49,1},{2,18}... | collective-permute-start | bytes 98312 | tf_op jit(solution)/shard_map/ppermute | solution.py:25
  59.9 20.2 %all-to-all-start.2 = ((f32[16,1,64,128]{3,2,1,0:T(8,128)}), f32[16,1,64,128]{3,2,1,0:T(8,128)S(1)}, u32[]{:S(2)}, u32[]{:S(2)}) async-start(f32[16,1,64,128]{3,2,1,0:T(8,128)} %stack.165), calls=%async_computation.2 | async-start | bytes 1048576 | tf_op jit(solution)/shard_map/all_to_all | solution.py:11
  64.7 5.2 %collective-permute-start.10 = (f32[64,128]{1,0:T(8,128)S(1)}, f32[64,128]{1,0:T(8,128)S(1)}, u32[]{:S(2)}, u32[]{:S(2)}) collective-permute-start(f32[64,128]{1,0:T(8,128)S(1)} %get-tuple-element.256), channel_id=1, source_target_pairs={{0,32},{16,48},{32,0},{48,16},{1,33},{17,49},{33,1},{49,17},{2,34}... | collective-permute-start | bytes 98312 | tf_op jit(solution)/shard_map/ppermute | solution.py:25
  84.8 20.2 %all-to-all-start.3 = ((f32[16,1,64,128]{3,2,1,0:T(8,128)}), f32[16,1,64,128]{3,2,1,0:T(8,128)S(1)}, u32[]{:S(2)}, u32[]{:S(2)}) async-start(f32[16,1,64,128]{3,2,1,0:T(8,128)} %stack.171), calls=%async_computation.3 | async-start | bytes 1048576 | tf_op jit(solution)/shard_map/all_to_all | solution.py:11
  89.7 5.2 %collective-permute-start.13 = (f32[64,128]{1,0:T(8,128)S(1)}, f32[64,128]{1,0:T(8,128)S(1)}, u32[]{:S(2)}, u32[]{:S(2)}) collective-permute-start(f32[64,128]{1,0:T(8,128)S(1)} %get-tuple-element.258), channel_id=1, source_target_pairs={{0,32},{16,48},{32,0},{48,16},{1,33},{17,49},{33,1},{49,17},{2,34}... | collective-permute-start | bytes 98312 | tf_op jit(solution)/shard_map/ppermute | solution.py:25
  109.7 20.2 %all-to-all-start.4 = ((f32[16,1,64,128]{3,2,1,0:T(8,128)}), f32[16,1,64,128]{3,2,1,0:T(8,128)S(1)}, u32[]{:S(2)}, u32[]{:S(2)}) async-start(f32[16,1,64,128]{3,2,1,0:T(8,128)} %stack.177), calls=%async_computation.4 | async-start | bytes 1048576 | tf_op jit(solution)/shard_map/all_to_all | solution.py:11
  114.6 5.2 %collective-permute-start.16 = (f32[64,128]{1,0:T(8,128)S(1)}, f32[64,128]{1,0:T(8,128)S(1)}, u32[]{:S(2)}, u32[]{:S(2)}) collective-permute-start(f32[64,128]{1,0:T(8,128)S(1)} %get-tuple-element.260), channel_id=1, source_target_pairs={{0,32},{16,48},{32,0},{48,16},{1,33},{17,49},{33,1},{49,17},{2,34}... | collective-permute-start | bytes 98312 | tf_op jit(solution)/shard_map/ppermute | solution.py:25
  134.7 20.2 %all-to-all-start.5 = ((f32[16,1,64,128]{3,2,1,0:T(8,128)}), f32[16,1,64,128]{3,2,1,0:T(8,128)S(1)}, u32[]{:S(2)}, u32[]{:S(2)}) async-start(f32[16,1,64,128]{3,2,1,0:T(8,128)} %stack.183), calls=%async_computation.5 | async-start | bytes 1048576 | tf_op jit(solution)/shard_map/all_to_all | solution.py:11
  138.1 5.1 %collective-permute-start.18 = (f32[64,128]{1,0:T(8,128)S(1)}, f32[64,128]{1,0:T(8,128)S(1)}, u32[]{:S(2)}, u32[]{:S(2)}) collective-permute-start(f32[64,128]{1,0:T(8,128)S(1)} %get-tuple-element.262), channel_id=1, source_target_pairs={{0,16},{16,32},{32,48},{48,0},{1,17},{17,33},{33,49},{49,1},{2,18}... | collective-permute-start | bytes 98312 | tf_op jit(solution)/shard_map/ppermute | solution.py:25
  139.5 5.2 %collective-permute-start.19 = (f32[64,128]{1,0:T(8,128)S(1)}, f32[64,128]{1,0:T(8,128)S(1)}, u32[]{:S(2)}, u32[]{:S(2)}) collective-permute-start(f32[64,128]{1,0:T(8,128)S(1)} %get-tuple-element.262), channel_id=1, source_target_pairs={{0,32},{16,48},{32,0},{48,16},{1,33},{17,49},{33,1},{49,17},{2,34}... | collective-permute-start | bytes 98312 | tf_op jit(solution)/shard_map/ppermute | solution.py:25
  159.7 20.2 %all-to-all-start.6 = ((f32[16,1,64,128]{3,2,1,0:T(8,128)}), f32[16,1,64,128]{3,2,1,0:T(8,128)S(1)}, u32[]{:S(2)}, u32[]{:S(2)}) async-start(f32[16,1,64,128]{3,2,1,0:T(8,128)} %stack.189), calls=%async_computation.6 | async-start | bytes 1048576 | tf_op jit(solution)/shard_map/all_to_all | solution.py:11
  163.1 5.1 %collective-permute-start.21 = (f32[64,128]{1,0:T(8,128)S(1)}, f32[64,128]{1,0:T(8,128)S(1)}, u32[]{:S(2)}, u32[]{:S(2)}) collective-permute-start(f32[64,128]{1,0:T(8,128)S(1)} %get-tuple-element.264), channel_id=1, source_target_pairs={{0,16},{16,32},{32,48},{48,0},{1,17},{17,33},{33,49},{49,1},{2,18}... | collective-permute-start | bytes 98312 | tf_op jit(solution)/shard_map/ppermute | solution.py:25
  164.5 5.2 %collective-permute-start.22 = (f32[64,128]{1,0:T(8,128)S(1)}, f32[64,128]{1,0:T(8,128)S(1)}, u32[]{:S(2)}, u32[]{:S(2)}) collective-permute-start(f32[64,128]{1,0:T(8,128)S(1)} %get-tuple-element.264), channel_id=1, source_target_pairs={{0,32},{16,48},{32,0},{48,16},{1,33},{17,49},{33,1},{49,17},{2,34}... | collective-permute-start | bytes 98312 | tf_op jit(solution)/shard_map/ppermute | solution.py:25
  184.6 20.2 %all-to-all-start.7 = ((f32[16,1,64,128]{3,2,1,0:T(8,128)}), f32[16,1,64,128]{3,2,1,0:T(8,128)S(1)}, u32[]{:S(2)}, u32[]{:S(2)}) async-start(f32[16,1,64,128]{3,2,1,0:T(8,128)} %stack.195), calls=%async_computation.7 | async-start | bytes 1048576 | tf_op jit(solution)/shard_map/all_to_all | solution.py:11
  188.1 5.1 %collective-permute-start.24 = (f32[64,128]{1,0:T(8,128)S(1)}, f32[64,128]{1,0:T(8,128)S(1)}, u32[]{:S(2)}, u32[]{:S(2)}) collective-permute-start(f32[64,128]{1,0:T(8,128)S(1)} %get-tuple-element.266), channel_id=1, source_target_pairs={{0,16},{16,32},{32,48},{48,0},{1,17},{17,33},{33,49},{49,1},{2,18}... | collective-permute-start | bytes 98312 | tf_op jit(solution)/shard_map/ppermute | solution.py:25
  189.4 5.2 %collective-permute-start.25 = (f32[64,128]{1,0:T(8,128)S(1)}, f32[64,128]{1,0:T(8,128)S(1)}, u32[]{:S(2)}, u32[]{:S(2)}) collective-permute-start(f32[64,128]{1,0:T(8,128)S(1)} %get-tuple-element.266), channel_id=1, source_target_pairs={{0,32},{16,48},{32,0},{48,16},{1,33},{17,49},{33,1},{49,17},{2,34}... | collective-permute-start | bytes 98312 | tf_op jit(solution)/shard_map/ppermute | solution.py:25
  212.7 20.2 %all-to-all-start = ((f32[16,64,128]{2,1,0:T(8,128)}), f32[16,64,128]{2,1,0:T(8,128)S(1)}, u32[]{:S(2)}, u32[]{:S(2)}) async-start(f32[16,64,128]{2,1,0:T(8,128)} %select_reduce_fusion.20), calls=%async_computation | async-start | bytes 1048576 | tf_op jit(solution)/shard_map/while/body/eval_jaxpr/all_to_all | solution.py:47
  216.3 16.6 %collective-permute-start = (f32[64,128]{1,0:T(8,128)S(1)}, f32[64,128]{1,0:T(8,128)S(1)}, u32[]{:S(2)}, u32[]{:S(2)}) collective-permute-start(f32[64,128]{1,0:T(8,128)S(1)} %get-tuple-element.323), channel_id=1, source_target_pairs={{0,48},{16,0},{32,16},{48,32},{1,49},{17,1},{33,17},{49,33},{2,50}... | collective-permute-start | bytes 98312 | tf_op jit(solution)/shard_map/while/body/eval_jaxpr/ppermute | solution.py:25
  219.1 13.8 %collective-permute-start.1 = (f32[64,128]{1,0:T(8,128)S(1)}, f32[64,128]{1,0:T(8,128)S(1)}, u32[]{:S(2)}, u32[]{:S(2)}) collective-permute-start(f32[64,128]{1,0:T(8,128)S(1)} %get-tuple-element.324), channel_id=1, source_target_pairs={{0,32},{16,48},{32,0},{48,16},{1,33},{17,49},{33,1},{49,17},{2,34}... | collective-permute-start | bytes 98312 | tf_op jit(solution)/shard_map/while/body/eval_jaxpr/ppermute | solution.py:25
  219.5 13.5 %collective-permute-start.2 = (f32[64,128]{1,0:T(8,128)S(1)}, f32[64,128]{1,0:T(8,128)S(1)}, u32[]{:S(2)}, u32[]{:S(2)}) collective-permute-start(f32[64,128]{1,0:T(8,128)S(1)} %get-tuple-element.325), channel_id=1, source_target_pairs={{0,16},{16,32},{32,48},{48,0},{1,17},{17,33},{33,49},{49,1},{2,18}... | collective-permute-start | bytes 98312 | tf_op jit(solution)/shard_map/while/body/eval_jaxpr/ppermute | solution.py:25
  236.9 20.2 %all-to-all-start = ((f32[16,64,128]{2,1,0:T(8,128)}), f32[16,64,128]{2,1,0:T(8,128)S(1)}, u32[]{:S(2)}, u32[]{:S(2)}) async-start(f32[16,64,128]{2,1,0:T(8,128)} %select_reduce_fusion.20), calls=%async_computation | async-start | bytes 1048576 | tf_op jit(solution)/shard_map/while/body/eval_jaxpr/all_to_all | solution.py:47
  240.5 16.6 %collective-permute-start = (f32[64,128]{1,0:T(8,128)S(1)}, f32[64,128]{1,0:T(8,128)S(1)}, u32[]{:S(2)}, u32[]{:S(2)}) collective-permute-start(f32[64,128]{1,0:T(8,128)S(1)} %get-tuple-element.323), channel_id=1, source_target_pairs={{0,48},{16,0},{32,16},{48,32},{1,49},{17,1},{33,17},{49,33},{2,50}... | collective-permute-start | bytes 98312 | tf_op jit(solution)/shard_map/while/body/eval_jaxpr/ppermute | solution.py:25
  243.3 13.8 %collective-permute-start.1 = (f32[64,128]{1,0:T(8,128)S(1)}, f32[64,128]{1,0:T(8,128)S(1)}, u32[]{:S(2)}, u32[]{:S(2)}) collective-permute-start(f32[64,128]{1,0:T(8,128)S(1)} %get-tuple-element.324), channel_id=1, source_target_pairs={{0,32},{16,48},{32,0},{48,16},{1,33},{17,49},{33,1},{49,17},{2,34}... | collective-permute-start | bytes 98312 | tf_op jit(solution)/shard_map/while/body/eval_jaxpr/ppermute | solution.py:25
  243.7 13.5 %collective-permute-start.2 = (f32[64,128]{1,0:T(8,128)S(1)}, f32[64,128]{1,0:T(8,128)S(1)}, u32[]{:S(2)}, u32[]{:S(2)}) collective-permute-start(f32[64,128]{1,0:T(8,128)S(1)} %get-tuple-element.325), channel_id=1, source_target_pairs={{0,16},{16,32},{32,48},{48,0},{1,17},{17,33},{33,49},{49,1},{2,18}... | collective-permute-start | bytes 98312 | tf_op jit(solution)/shard_map/while/body/eval_jaxpr/ppermute | solution.py:25
  261.0 20.2 %all-to-all-start = ((f32[16,64,128]{2,1,0:T(8,128)}), f32[16,64,128]{2,1,0:T(8,128)S(1)}, u32[]{:S(2)}, u32[]{:S(2)}) async-start(f32[16,64,128]{2,1,0:T(8,128)} %select_reduce_fusion.20), calls=%async_computation | async-start | bytes 1048576 | tf_op jit(solution)/shard_map/while/body/eval_jaxpr/all_to_all | solution.py:47
  264.7 16.6 %collective-permute-start = (f32[64,128]{1,0:T(8,128)S(1)}, f32[64,128]{1,0:T(8,128)S(1)}, u32[]{:S(2)}, u32[]{:S(2)}) collective-permute-start(f32[64,128]{1,0:T(8,128)S(1)} %get-tuple-element.323), channel_id=1, source_target_pairs={{0,48},{16,0},{32,16},{48,32},{1,49},{17,1},{33,17},{49,33},{2,50}... | collective-permute-start | bytes 98312 | tf_op jit(solution)/shard_map/while/body/eval_jaxpr/ppermute | solution.py:25
  267.5 13.8 %collective-permute-start.1 = (f32[64,128]{1,0:T(8,128)S(1)}, f32[64,128]{1,0:T(8,128)S(1)}, u32[]{:S(2)}, u32[]{:S(2)}) collective-permute-start(f32[64,128]{1,0:T(8,128)S(1)} %get-tuple-element.324), channel_id=1, source_target_pairs={{0,32},{16,48},{32,0},{48,16},{1,33},{17,49},{33,1},{49,17},{2,34}... | collective-permute-start | bytes 98312 | tf_op jit(solution)/shard_map/while/body/eval_jaxpr/ppermute | solution.py:25
  267.8 13.5 %collective-permute-start.2 = (f32[64,128]{1,0:T(8,128)S(1)}, f32[64,128]{1,0:T(8,128)S(1)}, u32[]{:S(2)}, u32[]{:S(2)}) collective-permute-start(f32[64,128]{1,0:T(8,128)S(1)} %get-tuple-element.325), channel_id=1, source_target_pairs={{0,16},{16,32},{32,48},{48,0},{1,17},{17,33},{33,49},{49,1},{2,18}... | collective-permute-start | bytes 98312 | tf_op jit(solution)/shard_map/while/body/eval_jaxpr/ppermute | solution.py:25
  285.2 20.2 %all-to-all-start = ((f32[16,64,128]{2,1,0:T(8,128)}), f32[16,64,128]{2,1,0:T(8,128)S(1)}, u32[]{:S(2)}, u32[]{:S(2)}) async-start(f32[16,64,128]{2,1,0:T(8,128)} %select_reduce_fusion.20), calls=%async_computation | async-start | bytes 1048576 | tf_op jit(solution)/shard_map/while/body/eval_jaxpr/all_to_all | solution.py:47
  288.8 16.6 %collective-permute-start = (f32[64,128]{1,0:T(8,128)S(1)}, f32[64,128]{1,0:T(8,128)S(1)}, u32[]{:S(2)}, u32[]{:S(2)}) collective-permute-start(f32[64,128]{1,0:T(8,128)S(1)} %get-tuple-element.323), channel_id=1, source_target_pairs={{0,48},{16,0},{32,16},{48,32},{1,49},{17,1},{33,17},{49,33},{2,50}... | collective-permute-start | bytes 98312 | tf_op jit(solution)/shard_map/while/body/eval_jaxpr/ppermute | solution.py:25
  291.6 13.8 %collective-permute-start.1 = (f32[64,128]{1,0:T(8,128)S(1)}, f32[64,128]{1,0:T(8,128)S(1)}, u32[]{:S(2)}, u32[]{:S(2)}) collective-permute-start(f32[64,128]{1,0:T(8,128)S(1)} %get-tuple-element.324), channel_id=1, source_target_pairs={{0,32},{16,48},{32,0},{48,16},{1,33},{17,49},{33,1},{49,17},{2,34}... | collective-permute-start | bytes 98312 | tf_op jit(solution)/shard_map/while/body/eval_jaxpr/ppermute | solution.py:25
  292.0 13.5 %collective-permute-start.2 = (f32[64,128]{1,0:T(8,128)S(1)}, f32[64,128]{1,0:T(8,128)S(1)}, u32[]{:S(2)}, u32[]{:S(2)}) collective-permute-start(f32[64,128]{1,0:T(8,128)S(1)} %get-tuple-element.325), channel_id=1, source_target_pairs={{0,16},{16,32},{32,48},{48,0},{1,17},{17,33},{33,49},{49,1},{2,18}... | collective-permute-start | bytes 98312 | tf_op jit(solution)/shard_map/while/body/eval_jaxpr/ppermute | solution.py:25
  309.4 20.2 %all-to-all-start = ((f32[16,64,128]{2,1,0:T(8,128)}), f32[16,64,128]{2,1,0:T(8,128)S(1)}, u32[]{:S(2)}, u32[]{:S(2)}) async-start(f32[16,64,128]{2,1,0:T(8,128)} %select_reduce_fusion.20), calls=%async_computation | async-start | bytes 1048576 | tf_op jit(solution)/shard_map/while/body/eval_jaxpr/all_to_all | solution.py:47
  313.0 16.6 %collective-permute-start = (f32[64,128]{1,0:T(8,128)S(1)}, f32[64,128]{1,0:T(8,128)S(1)}, u32[]{:S(2)}, u32[]{:S(2)}) collective-permute-start(f32[64,128]{1,0:T(8,128)S(1)} %get-tuple-element.323), channel_id=1, source_target_pairs={{0,48},{16,0},{32,16},{48,32},{1,49},{17,1},{33,17},{49,33},{2,50}... | collective-permute-start | bytes 98312 | tf_op jit(solution)/shard_map/while/body/eval_jaxpr/ppermute | solution.py:25
  315.8 13.8 %collective-permute-start.1 = (f32[64,128]{1,0:T(8,128)S(1)}, f32[64,128]{1,0:T(8,128)S(1)}, u32[]{:S(2)}, u32[]{:S(2)}) collective-permute-start(f32[64,128]{1,0:T(8,128)S(1)} %get-tuple-element.324), channel_id=1, source_target_pairs={{0,32},{16,48},{32,0},{48,16},{1,33},{17,49},{33,1},{49,17},{2,34}... | collective-permute-start | bytes 98312 | tf_op jit(solution)/shard_map/while/body/eval_jaxpr/ppermute | solution.py:25
  316.2 13.5 %collective-permute-start.2 = (f32[64,128]{1,0:T(8,128)S(1)}, f32[64,128]{1,0:T(8,128)S(1)}, u32[]{:S(2)}, u32[]{:S(2)}) collective-permute-start(f32[64,128]{1,0:T(8,128)S(1)} %get-tuple-element.325), channel_id=1, source_target_pairs={{0,16},{16,32},{32,48},{48,0},{1,17},{17,33},{33,49},{49,1},{2,18}... | collective-permute-start | bytes 98312 | tf_op jit(solution)/shard_map/while/body/eval_jaxpr/ppermute | solution.py:25
  333.6 20.2 %all-to-all-start = ((f32[16,64,128]{2,1,0:T(8,128)}), f32[16,64,128]{2,1,0:T(8,128)S(1)}, u32[]{:S(2)}, u32[]{:S(2)}) async-start(f32[16,64,128]{2,1,0:T(8,128)} %select_reduce_fusion.20), calls=%async_computation | async-start | bytes 1048576 | tf_op jit(solution)/shard_map/while/body/eval_jaxpr/all_to_all | solution.py:47
  337.2 16.6 %collective-permute-start = (f32[64,128]{1,0:T(8,128)S(1)}, f32[64,128]{1,0:T(8,128)S(1)}, u32[]{:S(2)}, u32[]{:S(2)}) collective-permute-start(f32[64,128]{1,0:T(8,128)S(1)} %get-tuple-element.323), channel_id=1, source_target_pairs={{0,48},{16,0},{32,16},{48,32},{1,49},{17,1},{33,17},{49,33},{2,50}... | collective-permute-start | bytes 98312 | tf_op jit(solution)/shard_map/while/body/eval_jaxpr/ppermute | solution.py:25
  340.0 13.8 %collective-permute-start.1 = (f32[64,128]{1,0:T(8,128)S(1)}, f32[64,128]{1,0:T(8,128)S(1)}, u32[]{:S(2)}, u32[]{:S(2)}) collective-permute-start(f32[64,128]{1,0:T(8,128)S(1)} %get-tuple-element.324), channel_id=1, source_target_pairs={{0,32},{16,48},{32,0},{48,16},{1,33},{17,49},{33,1},{49,17},{2,34}... | collective-permute-start | bytes 98312 | tf_op jit(solution)/shard_map/while/body/eval_jaxpr/ppermute | solution.py:25
  340.3 13.5 %collective-permute-start.2 = (f32[64,128]{1,0:T(8,128)S(1)}, f32[64,128]{1,0:T(8,128)S(1)}, u32[]{:S(2)}, u32[]{:S(2)}) collective-permute-start(f32[64,128]{1,0:T(8,128)S(1)} %get-tuple-element.325), channel_id=1, source_target_pairs={{0,16},{16,32},{32,48},{48,0},{1,17},{17,33},{33,49},{49,1},{2,18}... | collective-permute-start | bytes 98312 | tf_op jit(solution)/shard_map/while/body/eval_jaxpr/ppermute | solution.py:25
  357.7 20.2 %all-to-all-start = ((f32[16,64,128]{2,1,0:T(8,128)}), f32[16,64,128]{2,1,0:T(8,128)S(1)}, u32[]{:S(2)}, u32[]{:S(2)}) async-start(f32[16,64,128]{2,1,0:T(8,128)} %select_reduce_fusion.20), calls=%async_computation | async-start | bytes 1048576 | tf_op jit(solution)/shard_map/while/body/eval_jaxpr/all_to_all | solution.py:47
  361.4 16.6 %collective-permute-start = (f32[64,128]{1,0:T(8,128)S(1)}, f32[64,128]{1,0:T(8,128)S(1)}, u32[]{:S(2)}, u32[]{:S(2)}) collective-permute-start(f32[64,128]{1,0:T(8,128)S(1)} %get-tuple-element.323), channel_id=1, source_target_pairs={{0,48},{16,0},{32,16},{48,32},{1,49},{17,1},{33,17},{49,33},{2,50}... | collective-permute-start | bytes 98312 | tf_op jit(solution)/shard_map/while/body/eval_jaxpr/ppermute | solution.py:25
  364.2 13.8 %collective-permute-start.1 = (f32[64,128]{1,0:T(8,128)S(1)}, f32[64,128]{1,0:T(8,128)S(1)}, u32[]{:S(2)}, u32[]{:S(2)}) collective-permute-start(f32[64,128]{1,0:T(8,128)S(1)} %get-tuple-element.324), channel_id=1, source_target_pairs={{0,32},{16,48},{32,0},{48,16},{1,33},{17,49},{33,1},{49,17},{2,34}... | collective-permute-start | bytes 98312 | tf_op jit(solution)/shard_map/while/body/eval_jaxpr/ppermute | solution.py:25
  364.5 13.5 %collective-permute-start.2 = (f32[64,128]{1,0:T(8,128)S(1)}, f32[64,128]{1,0:T(8,128)S(1)}, u32[]{:S(2)}, u32[]{:S(2)}) collective-permute-start(f32[64,128]{1,0:T(8,128)S(1)} %get-tuple-element.325), channel_id=1, source_target_pairs={{0,16},{16,32},{32,48},{48,0},{1,17},{17,33},{33,49},{49,1},{2,18}... | collective-permute-start | bytes 98312 | tf_op jit(solution)/shard_map/while/body/eval_jaxpr/ppermute | solution.py:25
  (15 other events, 58.5 us)
